TPU v7x, 32 devices: a whole 2x2x4 slice. The times are simulated.
32 devices in a mesh: groups: 2 (over y), freq: 4 (over x, core), recv: 4 (over z).
Axes of the slice: x: 2, y: 2, z: 4, core: 2. Of those that a mesh axis runs over, the one named last changes fastest.
Arguments:
- operator: bfloat16 [4, 32, 512, 2048], P('groups', 'freq', 'recv'), parts along dimension 0, may hold values from -0.125 to 0.125
- recorded: float32 [4, 32, 8, 512], P('groups', 'freq', None, 'recv'), parts along dimension 0, may hold values from -18 to 18
- win_start: int32 [16, 16], P('groups'), parts along dimension 0, may hold values from 0 to 15
- win_end: int32 [16, 16], P('groups'), parts along dimension 0, may hold values from 17 to 32
Outputs:
- reflectivity: float32 [4, 32, 8, 2048], P('groups', 'freq', None, 'recv'), parts along dimension 0
- residual: float32 [4, 32, 8, 512], P('groups', 'freq', None, 'recv'), parts along dimension 0
There are 2 independent parts, one for each index of `groups`. A program takes and returns all parts, laid end to end along the dimension named above; each array names one. Nothing has to cross between parts.
All inputs are finite; a program needn't handle non-finite values.
Results may differ from a plain program's by a relative error of at most 0.013.
Values may be sent and summed in bfloat16 or wider, within the bound.
No kernel may reach another device: no remote copies, remote signals or barrier semaphores. Data moves between devices by JAX's collectives and lax.ppermute only.
A program may use at most 64 MiB of HBM per device.

v0:
```python
import math
import jax
import jax.numpy as jnp
from jax import lax
from jax.sharding import PartitionSpec as P

SBLK = 128
LINK_TYPE = jnp.float32
ITERS = 5


def high_dot(left, right):
    return jnp.dot(left, right, precision=lax.Precision.HIGHEST)


def dft_rows(row_ids, length):
    positions = jnp.arange(length, dtype=jnp.int32)
    phases = (row_ids[:, None] * positions[None, :] % length).astype(jnp.float32) * (
        2.0 * math.pi / length
    )
    normalizer = 1.0 / math.sqrt(length)
    return (jnp.cos(phases) * normalizer, jnp.sin(phases) * normalizer)


def window_mask(column_ids, src_local, win_start, win_end, length):
    blocks = win_start.shape[1]
    side_ids = column_ids // src_local
    source_ids = lax.axis_index("recv") * src_local + column_ids % src_local
    flat_ids = side_ids * blocks + source_ids // SBLK
    table_ids = jnp.arange(win_start.shape[0] * blocks, dtype=jnp.int32)
    matches = flat_ids[:, None] == table_ids[None, :]
    opening = jnp.sum(jnp.where(matches, win_start.reshape(-1)[None, :], 0), axis=1)
    closing = jnp.sum(jnp.where(matches, win_end.reshape(-1)[None, :], 0), axis=1)
    samples = jnp.arange(length, dtype=jnp.int32)[:, None]
    return ((samples >= opening[None, :]) & (samples < closing[None, :])).astype(jnp.float32)


def adjoint(res, real_operator, imag_operator):
    real_part = jnp.einsum(
        "fbr,frs->fbs", res[0], real_operator, preferred_element_type=jnp.float32
    ) + jnp.einsum("fbr,frs->fbs", res[1], imag_operator, preferred_element_type=jnp.float32)
    imag_part = jnp.einsum(
        "fbr,frs->fbs", res[1], real_operator, preferred_element_type=jnp.float32
    ) - jnp.einsum("fbr,frs->fbs", res[0], imag_operator, preferred_element_type=jnp.float32)
    return jnp.stack([real_part, imag_part])


def split_adjoint(values, real_operator, imag_operator):
    high, low = split_high_low(values)
    doubled = adjoint(jnp.concatenate([high, low], axis=2), real_operator, imag_operator)
    rows = values.shape[2]
    return doubled[:, :, :rows] + doubled[:, :, rows:]


def forward(direction, real_operator, imag_operator):
    real_part = jnp.einsum(
        "fbs,frs->fbr", direction[0], real_operator, preferred_element_type=jnp.float32
    ) - jnp.einsum("fbs,frs->fbr", direction[1], imag_operator, preferred_element_type=jnp.float32)
    imag_part = jnp.einsum(
        "fbs,frs->fbr", direction[0], imag_operator, preferred_element_type=jnp.float32
    ) + jnp.einsum("fbs,frs->fbr", direction[1], real_operator, preferred_element_type=jnp.float32)
    return jnp.stack([real_part, imag_part])


def split_high_low(values):
    high = lax.reduce_precision(values, exponent_bits=8, mantissa_bits=7)
    return (high.astype(jnp.bfloat16), (values - high).astype(jnp.bfloat16))


def split_parts(values):
    pieces = []
    for value in values:
        high = lax.reduce_precision(value, exponent_bits=8, mantissa_bits=7)
        rest = value - high
        middle = lax.reduce_precision(rest, exponent_bits=8, mantissa_bits=7)
        pieces += [high, middle, rest - middle]
    return jnp.stack(pieces)


def reduce_gather(partial):
    scattered = lax.psum_scatter(partial.astype(LINK_TYPE), "recv", scatter_dimension=3, tiled=True)
    flat = scattered.reshape(scattered.shape[0], scattered.shape[1], -1)
    return lax.all_gather(flat, "freq", axis=1, tiled=True).astype(jnp.float32)


def gather_sources(block, values):
    src_local = block.shape[-1]
    recv_size = lax.axis_size("recv")
    rows = jnp.concatenate(split_high_low(block.reshape(-1, src_local)))
    pieces = split_parts(values)
    extra = jnp.zeros((16, src_local), jnp.float32).at[0, : pieces.shape[0]].set(pieces)
    payload = jnp.concatenate([rows, extra.astype(jnp.bfloat16)])
    gathered = lax.all_gather(payload, "recv", axis=1, tiled=True)
    count = rows.shape[0]
    half = count // 2
    joined = gathered[:half].astype(jnp.float32) + gathered[half:count].astype(jnp.float32)
    full = joined.reshape(block.shape[:-1] + (recv_size * src_local,))
    tail = gathered[count].reshape(recv_size, src_local)[:, : pieces.shape[0]].astype(jnp.float32)
    sums = jnp.sum(tail.reshape(recv_size, len(values), 3), axis=(0, 2))
    return (full, sums)


def on_device(operator, recorded, win_start, win_end):
    freq_local = operator.shape[1]
    sources = operator.shape[3]
    right_sides = recorded.shape[2]
    src_local = sources // lax.axis_size("recv")
    total_freq = freq_local * lax.axis_size("freq")
    columns = right_sides * src_local
    real_operator = operator[0]
    imag_operator = operator[1]
    cos_all, sin_all = dft_rows(jnp.arange(total_freq, dtype=jnp.int32), total_freq)
    own_rows = lax.axis_index("freq") * freq_local + jnp.arange(freq_local, dtype=jnp.int32)
    cos_own, sin_own = dft_rows(own_rows, total_freq)
    window = window_mask(
        jnp.arange(columns, dtype=jnp.int32), src_local, win_start, win_end, total_freq
    )
    block_shape = (2, freq_local, right_sides, src_local)

    def to_time(spectrum):
        time_real = high_dot(cos_all.T, spectrum[0]) - high_dot(sin_all.T, spectrum[1])
        time_imag = high_dot(sin_all.T, spectrum[0]) + high_dot(cos_all.T, spectrum[1])
        return (time_real, time_imag)

    def to_own_freq(kept_real, kept_imag):
        real_part = high_dot(cos_own, kept_real) + high_dot(sin_own, kept_imag)
        imag_part = high_dot(cos_own, kept_imag) - high_dot(sin_own, kept_real)
        return jnp.stack([real_part, imag_part]).reshape(block_shape)

    gradient = reduce_gather(split_adjoint(recorded, real_operator, imag_operator))
    time_real, time_imag = to_time(gradient)
    kept_real = time_real * window
    kept_imag = time_imag * window
    kept_power = jnp.sum(kept_real * kept_real + kept_imag * kept_imag)
    direction_own = to_own_freq(kept_real, kept_imag)
    direction_all, sums = gather_sources(direction_own, [kept_power])
    direction_power = sums[0]
    reflect = jnp.zeros(block_shape, jnp.float32)
    residual = recorded
    for iteration in range(ITERS):
        image = forward(direction_all.astype(jnp.bfloat16), real_operator, imag_operator)
        if iteration < ITERS - 1:
            normal = reduce_gather(split_adjoint(image, real_operator, imag_operator))
            normal_real, normal_imag = to_time(normal)
            image_part = jnp.sum(kept_real * normal_real + kept_imag * normal_imag)
            masked_real = normal_real * window
            masked_imag = normal_imag * window
            change_own = to_own_freq(masked_real, masked_imag)
            values = [image_part] if iteration == 0 else [image_part, kept_power]
            change_all, sums = gather_sources(change_own, values)
            image_energy = sums[0]
            if iteration > 0:
                direction_power = sums[1]
            step_length = direction_power / (image_energy + 1e-06)
            reflect = reflect + step_length * direction_own
            residual = residual - step_length * image
            direction_all = direction_all - step_length * change_all
            direction_own = direction_own - step_length * change_own
            kept_real = kept_real - step_length * masked_real
            kept_imag = kept_imag - step_length * masked_imag
            kept_power = jnp.sum(kept_real * kept_real + kept_imag * kept_imag)
        else:
            own_power = jnp.where(lax.axis_index("freq") == 0, kept_power, 0.0)
            direction_power, image_energy = lax.psum(
                (own_power, jnp.sum(image * image)), ("freq", "recv")
            )
            step_length = direction_power / (image_energy + 1e-06)
            reflect = reflect + step_length * direction_own
            residual = residual - step_length * image
    return (reflect, residual)


def solution(mesh):
    return jax.shard_map(
        on_device,
        mesh=mesh,
        in_specs=(
            P("groups", "freq", "recv", None),
            P("groups", "freq", None, "recv"),
            P("groups", None),
            P("groups", None),
        ),
        out_specs=(P("groups", "freq", None, "recv"), P("groups", "freq", None, "recv")),
        check_vma=False,
    )
```

profile of v0, /device:TPU:0, one launch (start us, length us, event | category | flops | bytes accessed | tf_op | source)
XLA Modules:
  0.0 635.1 jit_solution(10183816585812269567)
XLA Ops:
  8.1 3.0 fusion.38
  11.1 3.4 fusion.40
  17.0 29.9 %reduce-scatter.6.cloned.1.call-done = f32[2,8,8,512]{3,2,1,0:T(8,128)} async-done(((f32[2,8,8,2048]{3,2,1,0:T(8,128)}), f32[2,8,8,512]{3,2,1,0:T(8,128)}) %reduce-scatter.6.cloned.1.call-update) | async-done | bytes 262160 | tf_op jit(solution)/shard_map/reduce_scatter | solution.py:81
  46.9 1.7 reshape.281
  48.9 1.8 select_reduce_fusion.1
  50.8 13.8 %all-gather.11.cloned.1.call-done = f32[2,32,4096]{2,1,0:T(8,128)} async-done(((f32[2,8,4096]{2,1,0:T(8,128)}), f32[2,32,4096]{2,1,0:T(8,128)}) %all-gather.11.cloned.1.call-update) | async-done | bytes 1048592 | tf_op jit(solution)/shard_map/all_gather | solution.py:83
  64.6 1.7 fusion.219
  66.3 1.7 fusion.220
  68.0 1.8 fusion.1
  69.9 2.5 add_reduce_fusion.8
  80.4 28.9 %all-gather.13.cloned.1.call-done = bf16[272,2048]{1,0:T(8,128)(2,1)} async-done(((bf16[272,512]{1,0:T(8,128)(2,1)}), bf16[272,2048]{1,0:T(8,128)(2,1)}) %all-gather.13.cloned.1.call-update) | async-done | bytes 1114128 | tf_op jit(solution)/shard_map/all_gather | solution.py:93
  110.6 3.5 fusion.34
  114.1 3.4 fusion.36
  117.5 3.5 fusion.151
  121.1 3.4 fusion.145
  128.4 26.7 %reduce-scatter.8.cloned.1.call-done = f32[2,8,8,512]{3,2,1,0:T(8,128)} async-done(((f32[2,8,8,2048]{3,2,1,0:T(8,128)}), f32[2,8,8,512]{3,2,1,0:T(8,128)}) %reduce-scatter.8.cloned.1.call-update) | async-done | bytes 262160 | tf_op jit(solution)/shard_map/reduce_scatter | solution.py:81
  155.2 1.7 reshape.283
  156.9 15.6 %all-gather.15.cloned.1.call-done = f32[2,32,4096]{2,1,0:T(8,128)} async-done(((f32[2,8,4096]{2,1,0:T(8,128)}), f32[2,32,4096]{2,1,0:T(8,128)}) %all-gather.15.cloned.1.call-update) | async-done | bytes 1048592 | tf_op jit(solution)/shard_map/all_gather | solution.py:83
  172.5 1.7 fusion.221
  174.3 1.7 fusion.222
  176.0 1.7 convolution_subtract_fusion.3
  177.8 2.4 add_reduce_fusion.7
  190.7 27.3 %all-gather.17.cloned.1.call-done = bf16[272,2048]{1,0:T(8,128)(2,1)} async-done(((bf16[272,512]{1,0:T(8,128)(2,1)}), bf16[272,2048]{1,0:T(8,128)(2,1)}) %all-gather.17.cloned.1.call-update) | async-done | bytes 1114128 | tf_op jit(solution)/shard_map/all_gather | solution.py:93
  220.7 2.0 fusion.606
  222.8 3.4 fusion.26
  226.2 3.5 fusion.28
  229.7 3.4 fusion.163
  238.3 26.7 %reduce-scatter.10.cloned.1.call-done = f32[2,8,8,512]{3,2,1,0:T(8,128)} async-done(((f32[2,8,8,2048]{3,2,1,0:T(8,128)}), f32[2,8,8,512]{3,2,1,0:T(8,128)}) %reduce-scatter.10.cloned.1.call-update) | async-done | bytes 262160 | tf_op jit(solution)/shard_map/reduce_scatter | solution.py:81
  265.0 1.7 reshape.285
  266.8 15.9 %all-gather.19.cloned.1.call-done = f32[2,32,4096]{2,1,0:T(8,128)} async-done(((f32[2,8,4096]{2,1,0:T(8,128)}), f32[2,32,4096]{2,1,0:T(8,128)}) %all-gather.19.cloned.1.call-update) | async-done | bytes 1048592 | tf_op jit(solution)/shard_map/all_gather | solution.py:83
  282.6 1.7 fusion.223
  284.4 1.7 fusion.224
  286.1 1.8 convolution_subtract_fusion.2
  287.9 3.9 add_reduce_fusion.5
  307.4 28.9 %all-gather.21.cloned.1.call-done = bf16[272,2048]{1,0:T(8,128)(2,1)} async-done(((bf16[272,512]{1,0:T(8,128)(2,1)}), bf16[272,2048]{1,0:T(8,128)(2,1)}) %all-gather.21.cloned.1.call-update) | async-done | bytes 1114128 | tf_op jit(solution)/shard_map/all_gather | solution.py:93
  340.8 3.4 fusion.18
  344.2 3.5 fusion.20
  347.8 3.4 fusion.175
  356.3 26.7 %reduce-scatter.12.cloned.1.call-done = f32[2,8,8,512]{3,2,1,0:T(8,128)} async-done(((f32[2,8,8,2048]{3,2,1,0:T(8,128)}), f32[2,8,8,512]{3,2,1,0:T(8,128)}) %reduce-scatter.12.cloned.1.call-update) | async-done | bytes 262160 | tf_op jit(solution)/shard_map/reduce_scatter | solution.py:81
  383.1 1.7 reshape.287
  384.9 15.8 %all-gather.23.cloned.1.call-done = f32[2,32,4096]{2,1,0:T(8,128)} async-done(((f32[2,8,4096]{2,1,0:T(8,128)}), f32[2,32,4096]{2,1,0:T(8,128)}) %all-gather.23.cloned.1.call-update) | async-done | bytes 1048592 | tf_op jit(solution)/shard_map/all_gather | solution.py:83
  400.6 1.7 fusion.225
  402.4 1.7 fusion.226
  404.1 1.7 convolution_subtract_fusion.1
  405.9 3.9 add_reduce_fusion.3
  422.7 28.9 %all-gather.25.cloned.1.call-done = bf16[272,2048]{1,0:T(8,128)(2,1)} async-done(((bf16[272,512]{1,0:T(8,128)(2,1)}), bf16[272,2048]{1,0:T(8,128)(2,1)}) %all-gather.25.cloned.1.call-update) | async-done | bytes 1114128 | tf_op jit(solution)/shard_map/all_gather | solution.py:93
  454.6 2.1 fusion.605
  456.7 3.5 fusion.10
  460.2 3.4 fusion.12
  463.6 3.4 fusion.187
  472.2 26.7 %reduce-scatter.14.cloned.1.call-done = f32[2,8,8,512]{3,2,1,0:T(8,128)} async-done(((f32[2,8,8,2048]{3,2,1,0:T(8,128)}), f32[2,8,8,512]{3,2,1,0:T(8,128)}) %reduce-scatter.14.cloned.1.call-update) | async-done | bytes 262160 | tf_op jit(solution)/shard_map/reduce_scatter | solution.py:81
  498.9 1.7 reshape.289
  500.9 15.5 %all-gather.27.cloned.1.call-done = f32[2,32,4096]{2,1,0:T(8,128)} async-done(((f32[2,8,4096]{2,1,0:T(8,128)}), f32[2,32,4096]{2,1,0:T(8,128)}) %all-gather.27.cloned.1.call-update) | async-done | bytes 1048592 | tf_op jit(solution)/shard_map/all_gather | solution.py:83
  516.4 1.7 fusion.227
  518.1 1.7 fusion.228
  519.9 1.7 convolution_subtract_fusion
  521.6 3.9 add_reduce_fusion.1
  541.3 1.7 fusion.233
  547.1 25.1 %all-gather.29.cloned.1.call-done = bf16[272,2048]{1,0:T(8,128)(2,1)} async-done(((bf16[272,512]{1,0:T(8,128)(2,1)}), bf16[272,2048]{1,0:T(8,128)(2,1)}) %all-gather.29.cloned.1.call-update) | async-done | bytes 1114128 | tf_op jit(solution)/shard_map/all_gather | solution.py:93
  576.6 3.4 fusion.2
  579.9 3.4 fusion.4
  583.3 3.5 fusion.199
  586.9 3.5 fusion.193
  592.7 32.6 %all-reduce.5 = (f32[]{:T(128)}, f32[]{:T(128)}) all-reduce(f32[]{:T(128)S(6)} %select_n.95, f32[]{:T(128)} %multiply_reduce_fusion), channel_id=1, replica_groups=mesh['groups'=2,'freq'=4,'recv'=4] {'freq','recv'}, use_global_device_ids=true, to_apply=%region_24.25 | all-reduce | flops 2 | bytes 16 | tf_op jit(solution)/shard_map/psum | solution.py:164
  (244 shorter events, 64.8 us)
Async XLA Ops:
  7.2 39.8 %reduce-scatter.6.cloned.1.call-start = ((), (), s32[]{:S(2)}) async-start(), calls=%async_computation.5 | async-start | bytes 1310720 | tf_op jit(solution)/shard_map/reduce_scatter | solution.py:81
  8.1 6.4 %copy-start = (bf16[2,8,128,2048]{3,2,1,0:T(8,128)(2,1)S(1)}, bf16[2,8,128,2048]{3,2,1,0:T(8,128)(2,1)}, u32[]{:S(2)}) copy-start(bf16[2,8,128,2048]{3,2,1,0:T(8,128)(2,1)} %param.14) | copy-start | bytes 25165828
  15.1 33.6 %copy-start.35 = (s32[8,16]{1,0:T(8,128)S(1)}, s32[8,16]{1,0:T(8,128)}, u32[]{:S(2)}) copy-start(s32[8,16]{1,0:T(8,128)} %param.16) | copy-start | bytes 1540
  15.1 33.7 %copy-start.36 = (s32[8,16]{1,0:T(8,128)S(1)}, s32[8,16]{1,0:T(8,128)}, u32[]{:S(2)}) copy-start(s32[8,16]{1,0:T(8,128)} %param.17) | copy-start | bytes 1540
  16.9 47.6 %all-gather.11.cloned.1.call-start = ((), (), s32[]{:S(2)}) async-start(), calls=%async_computation.6 | async-start | bytes 1310720 | tf_op jit(solution)/shard_map/all_gather | solution.py:83
  48.6 60.6 %all-gather.13.cloned.1.call-start = ((), (), s32[]{:S(2)}) async-start(), calls=%async_computation.7 | async-start | bytes 1392640 | tf_op jit(solution)/shard_map/all_gather | solution.py:93
  80.1 75.0 %reduce-scatter.8.cloned.1.call-start = ((), (), s32[]{:S(2)}) async-start(), calls=%async_computation.8 | async-start | bytes 1310720 | tf_op jit(solution)/shard_map/reduce_scatter | solution.py:81
  110.6 13.9 %slice-start = ((s8[8388608]{0:T(1024)(128)(4,1)}), s8[4194304]{0:T(1024)(128)(4,1)S(1)}, s32[]{:S(2)}) async-start(s8[8388608]{0:T(1024)(128)(4,1)} %bitcast.400), calls=%async_computation.20 | async-start | bytes 8388608
  117.5 7.0 %slice-start.1 = ((s8[8388608]{0:T(1024)(128)(4,1)}), s8[4194304]{0:T(1024)(128)(4,1)S(1)}, s32[]{:S(2)}) async-start(s8[8388608]{0:T(1024)(128)(4,1)} %bitcast.400), calls=%async_computation.21 | async-start | bytes 8388608
  128.4 44.2 %all-gather.15.cloned.1.call-start = ((), (), s32[]{:S(2)}) async-start(), calls=%async_computation.9 | async-start | bytes 1310720 | tf_op jit(solution)/shard_map/all_gather | solution.py:83
  156.9 61.1 %all-gather.17.cloned.1.call-start = ((), (), s32[]{:S(2)}) async-start(), calls=%async_computation.10 | async-start | bytes 1392640 | tf_op jit(solution)/shard_map/all_gather | solution.py:93
  180.2 42.6 %copy-start.2 = (f32[32,4096]{1,0:T(8,128)}, f32[32,4096]{1,0:T(8,128)S(1)}, u32[]{:S(2)}) copy-start(f32[32,4096]{1,0:T(8,128)S(1)} %get-tuple-element.111) | copy-start | bytes 1572868
  186.7 0.6 copy-start.5
  187.2 0.7 copy-start.7
  188.8 76.2 %reduce-scatter.10.cloned.1.call-start = ((), (), s32[]{:S(2)}) async-start(), calls=%async_computation.11 | async-start | bytes 1310720 | tf_op jit(solution)/shard_map/reduce_scatter | solution.py:81
  220.7 12.4 %slice-start.2 = ((s8[8388608]{0:T(1024)(128)(4,1)}), s8[4194304]{0:T(1024)(128)(4,1)S(1)}, s32[]{:S(2)}) async-start(s8[8388608]{0:T(1024)(128)(4,1)} %bitcast.402), calls=%async_computation.22 | async-start | bytes 8388608
  226.2 6.9 %slice-start.3 = ((s8[8388608]{0:T(1024)(128)(4,1)}), s8[4194304]{0:T(1024)(128)(4,1)S(1)}, s32[]{:S(2)}) async-start(s8[8388608]{0:T(1024)(128)(4,1)} %bitcast.402), calls=%async_computation.23 | async-start | bytes 8388608
  234.3 1.4 copy-start.24
  238.2 44.4 %all-gather.19.cloned.1.call-start = ((), (), s32[]{:S(2)}) async-start(), calls=%async_computation.12 | async-start | bytes 1310720 | tf_op jit(solution)/shard_map/all_gather | solution.py:83
  266.7 69.6 %all-gather.21.cloned.1.call-start = ((), (), s32[]{:S(2)}) async-start(), calls=%async_computation.13 | async-start | bytes 1392640 | tf_op jit(solution)/shard_map/all_gather | solution.py:93
  304.5 39.7 %copy-start.9 = (f32[8,4096]{1,0:T(8,128)}, f32[8,4096]{1,0:T(8,128)S(1)}, u32[]{:S(2)}) copy-start(f32[8,4096]{1,0:T(8,128)S(1)} %convolution_subtract_fusion.7) | copy-start | bytes 393220
  306.2 38.1 %copy-start.11 = (f32[8,4096]{1,0:T(8,128)}, f32[8,4096]{1,0:T(8,128)S(1)}, u32[]{:S(2)}) copy-start(f32[8,4096]{1,0:T(8,128)S(1)} %convolution_add_fusion.7) | copy-start | bytes 393220
  307.2 75.9 %reduce-scatter.12.cloned.1.call-start = ((), (), s32[]{:S(2)}) async-start(), calls=%async_computation.14 | async-start | bytes 1310720 | tf_op jit(solution)/shard_map/reduce_scatter | solution.py:81
  339.3 11.9 %slice-start.4 = ((s8[8388608]{0:T(1024)(128)(4,1)}), s8[4194304]{0:T(1024)(128)(4,1)S(1)}, s32[]{:S(2)}) async-start(s8[8388608]{0:T(1024)(128)(4,1)} %bitcast.404), calls=%async_computation.24 | async-start | bytes 8388608
  344.2 6.9 %slice-start.5 = ((s8[8388608]{0:T(1024)(128)(4,1)}), s8[4194304]{0:T(1024)(128)(4,1)S(1)}, s32[]{:S(2)}) async-start(s8[8388608]{0:T(1024)(128)(4,1)} %bitcast.404), calls=%async_computation.25 | async-start | bytes 8388608
  351.2 1.9 copy-start.26
  352.4 1.4 copy-start.28
  355.1 50.7 %copy-start.1 = (f32[32,4096]{1,0:T(8,128)S(1)}, f32[32,4096]{1,0:T(8,128)}, u32[]{:S(2)}) copy-start(f32[32,4096]{1,0:T(8,128)} %get-tuple-element.112) | copy-start | bytes 1572868
  356.3 44.3 %all-gather.23.cloned.1.call-start = ((), (), s32[]{:S(2)}) async-start(), calls=%async_computation.15 | async-start | bytes 1310720 | tf_op jit(solution)/shard_map/all_gather | solution.py:83
  384.8 66.8 %all-gather.25.cloned.1.call-start = ((), (), s32[]{:S(2)}) async-start(), calls=%async_computation.16 | async-start | bytes 1392640 | tf_op jit(solution)/shard_map/all_gather | solution.py:93
  420.9 33.6 %copy-start.13 = (f32[8,4096]{1,0:T(8,128)}, f32[8,4096]{1,0:T(8,128)S(1)}, u32[]{:S(2)}) copy-start(f32[8,4096]{1,0:T(8,128)S(1)} %convolution_subtract_fusion.6) | copy-start | bytes 393220
  421.5 33.1 %copy-start.15 = (f32[8,4096]{1,0:T(8,128)}, f32[8,4096]{1,0:T(8,128)S(1)}, u32[]{:S(2)}) copy-start(f32[8,4096]{1,0:T(8,128)S(1)} %convolution_add_fusion.6) | copy-start | bytes 393220
  422.4 76.4 %reduce-scatter.14.cloned.1.call-start = ((), (), s32[]{:S(2)}) async-start(), calls=%async_computation.17 | async-start | bytes 1310720 | tf_op jit(solution)/shard_map/reduce_scatter | solution.py:81
  454.6 12.4 %slice-start.6 = ((s8[8388608]{0:T(1024)(128)(4,1)}), s8[4194304]{0:T(1024)(128)(4,1)S(1)}, s32[]{:S(2)}) async-start(s8[8388608]{0:T(1024)(128)(4,1)} %bitcast.406), calls=%async_computation.26 | async-start | bytes 8388608
  456.6 10.3 %slice-start.7 = ((s8[8388608]{0:T(1024)(128)(4,1)}), s8[4194304]{0:T(1024)(128)(4,1)S(1)}, s32[]{:S(2)}) async-start(s8[8388608]{0:T(1024)(128)(4,1)} %bitcast.406), calls=%async_computation.27 | async-start | bytes 8388608
  467.0 1.9 copy-start.30
  468.2 1.4 copy-start.32
  472.1 44.3 %all-gather.27.cloned.1.call-start = ((), (), s32[]{:S(2)}) async-start(), calls=%async_computation.18 | async-start | bytes 1310720 | tf_op jit(solution)/shard_map/all_gather | solution.py:83
  500.6 71.6 %all-gather.29.cloned.1.call-start = ((), (), s32[]{:S(2)}) async-start(), calls=%async_computation.19 | async-start | bytes 1392640 | tf_op jit(solution)/shard_map/all_gather | solution.py:93
  525.6 17.7 %copy-start.6 = (f32[8,4096]{1,0:T(8,128)S(1)}, f32[8,4096]{1,0:T(8,128)}, u32[]{:S(2)}) copy-start(f32[8,4096]{1,0:T(8,128)} %copy-done.5) | copy-start | bytes 393220
  525.6 17.8 %copy-start.8 = (f32[8,4096]{1,0:T(8,128)S(1)}, f32[8,4096]{1,0:T(8,128)}, u32[]{:S(2)}) copy-start(f32[8,4096]{1,0:T(8,128)} %copy-done.7) | copy-start | bytes 393220
  525.6 17.9 %copy-start.10 = (f32[8,4096]{1,0:T(8,128)S(1)}, f32[8,4096]{1,0:T(8,128)}, u32[]{:S(2)}) copy-start(f32[8,4096]{1,0:T(8,128)} %copy-done.9) | copy-start | bytes 393220
  525.6 18.6 %copy-start.12 = (f32[8,4096]{1,0:T(8,128)S(1)}, f32[8,4096]{1,0:T(8,128)}, u32[]{:S(2)}) copy-start(f32[8,4096]{1,0:T(8,128)} %copy-done.11) | copy-start | bytes 393220
  525.6 19.3 %copy-start.14 = (f32[8,4096]{1,0:T(8,128)S(1)}, f32[8,4096]{1,0:T(8,128)}, u32[]{:S(2)}) copy-start(f32[8,4096]{1,0:T(8,128)} %copy-done.13) | copy-start | bytes 393220
  525.6 20.1 %copy-start.16 = (f32[8,4096]{1,0:T(8,128)S(1)}, f32[8,4096]{1,0:T(8,128)}, u32[]{:S(2)}) copy-start(f32[8,4096]{1,0:T(8,128)} %copy-done.15) | copy-start | bytes 393220
  543.2 3.1 copy-start.17
  583.3 7.1 %copy-start.3 = (f32[32,4096]{1,0:T(8,128)S(1)}, f32[32,4096]{1,0:T(8,128)}, u32[]{:S(2)}) copy-start(f32[32,4096]{1,0:T(8,128)} %get-tuple-element.72) | copy-start | bytes 1572868
  583.3 7.1 %copy-start.4 = (f32[32,4096]{1,0:T(8,128)S(1)}, f32[32,4096]{1,0:T(8,128)}, u32[]{:S(2)}) copy-start(f32[32,4096]{1,0:T(8,128)} %get-tuple-element.73) | copy-start | bytes 1572868
  586.8 39.7 %copy-start.25 = (f32[1,8,8,128]{3,2,1,0:T(8,128)S(1)}, f32[1,8,8,128]{3,2,1,0:T(8,128)}, u32[]{:S(2)}) copy-start(f32[1,8,8,128]{3,2,1,0:T(8,128)} %copy-done.24) | copy-start | bytes 98308
  586.8 39.7 %copy-start.27 = (f32[1,8,8,128]{3,2,1,0:T(8,128)S(1)}, f32[1,8,8,128]{3,2,1,0:T(8,128)}, u32[]{:S(2)}) copy-start(f32[1,8,8,128]{3,2,1,0:T(8,128)} %copy-done.26) | copy-start | bytes 98308
  586.8 39.7 %copy-start.29 = (f32[1,8,8,128]{3,2,1,0:T(8,128)S(1)}, f32[1,8,8,128]{3,2,1,0:T(8,128)}, u32[]{:S(2)}) copy-start(f32[1,8,8,128]{3,2,1,0:T(8,128)} %copy-done.28) | copy-start | bytes 98308
  586.8 39.7 %copy-start.31 = (f32[1,8,8,128]{3,2,1,0:T(8,128)S(1)}, f32[1,8,8,128]{3,2,1,0:T(8,128)}, u32[]{:S(2)}) copy-start(f32[1,8,8,128]{3,2,1,0:T(8,128)} %copy-done.30) | copy-start | bytes 98308
  586.8 39.7 %copy-start.33 = (f32[1,8,8,128]{3,2,1,0:T(8,128)S(1)}, f32[1,8,8,128]{3,2,1,0:T(8,128)}, u32[]{:S(2)}) copy-start(f32[1,8,8,128]{3,2,1,0:T(8,128)} %copy-done.32) | copy-start | bytes 98308
  586.8 39.7 %copy-start.34 = (f32[2,8,8,128]{3,2,1,0:T(8,128)S(1)}, f32[2,8,8,128]{3,2,1,0:T(8,128)}, u32[]{:S(2)}) copy-start(f32[2,8,8,128]{3,2,1,0:T(8,128)} %param.15) | copy-start | bytes 196612
  586.9 40.3 %copy-start.18 = (f32[2,8,8,512]{3,2,1,0:T(8,128)S(1)}, f32[2,8,8,512]{3,2,1,0:T(8,128)}, u32[]{:S(2)}) copy-start(f32[2,8,8,512]{3,2,1,0:T(8,128)} %copy-done.17) | copy-start | bytes 786436
  586.9 40.3 %copy-start.19 = (f32[1,8,8,512]{3,2,1,0:T(8,128)S(1)}, f32[1,8,8,512]{3,2,1,0:T(8,128)}, u32[]{:S(2)}) copy-start(f32[1,8,8,512]{3,2,1,0:T(8,128)} %copy.21) | copy-start | bytes 393220
  586.9 40.3 %copy-start.20 = (f32[1,8,8,512]{3,2,1,0:T(8,128)S(1)}, f32[1,8,8,512]{3,2,1,0:T(8,128)}, u32[]{:S(2)}) copy-start(f32[1,8,8,512]{3,2,1,0:T(8,128)} %copy.20) | copy-start | bytes 393220
  586.9 40.3 %copy-start.21 = (f32[1,8,8,512]{3,2,1,0:T(8,128)S(1)}, f32[1,8,8,512]{3,2,1,0:T(8,128)}, u32[]{:S(2)}) copy-start(f32[1,8,8,512]{3,2,1,0:T(8,128)} %copy.23) | copy-start | bytes 393220
  586.9 40.3 %copy-start.22 = (f32[1,8,8,512]{3,2,1,0:T(8,128)S(1)}, f32[1,8,8,512]{3,2,1,0:T(8,128)}, u32[]{:S(2)}) copy-start(f32[1,8,8,512]{3,2,1,0:T(8,128)} %copy.22) | copy-start | bytes 393220
  586.9 40.3 %copy-start.23 = (f32[1,8,8,512]{3,2,1,0:T(8,128)S(1)}, f32[1,8,8,512]{3,2,1,0:T(8,128)}, u32[]{:S(2)}) copy-start(f32[1,8,8,512]{3,2,1,0:T(8,128)} %copy.25) | copy-start | bytes 393220
Sparse Core Ops, SparseCore 0:
  17.1 29.8 reduce-scatter.5
  49.1 15.3 all-gather.10
  80.2 29.0 all-gather.12
  128.5 26.6 reduce-scatter.7
  157.1 15.3 all-gather.14
  189.0 29.0 all-gather.16
  238.3 26.6 reduce-scatter.9
  267.2 15.3 all-gather.18
  307.3 29.0 all-gather.20
  356.4 26.6 reduce-scatter.11
  385.2 15.3 all-gather.22
  422.6 29.0 all-gather.24
  472.2 26.6 reduce-scatter.13
  501.0 15.3 all-gather.26
  543.2 29.0 all-gather.28
where the time goes:
time: 644 us; the launch traced here: 635 us
  waiting for transfers between devices  353 us (55%)
  matrix products  136 us (21%)
  between operations  61.4 us (10%)
  blocking collectives  32.6 us (5%)
  other arithmetic  28.9 us (4%)
  local copies, waits for them, and re-layouts  21.9 us (3%)
    all_gather x5, waiting for transfers between devices, gather_sources(): gathered = lax.all_gather(payload, 'recv', axis=1, tiled=True)  139 us
    reduce_scatter x5, waiting for transfers between devices, reduce_gather(): lax.psum_scatter(partial.astype(LINK_TYPE), 'recv', scatter_dimension=3,...  137 us
    all_gather x5, waiting for transfers between devices, reduce_gather(): return lax.all_gather(flat, 'freq', axis=1, tiled=True).astype(jnp.float32)  76.5 us
    dot_general x40, matrix products, high_dot(): return jnp.dot(left, right, precision=lax.Precision.HIGHEST)  55 us
    psum x1, blocking collectives, on_device(): lax.psum((own_power, jnp.sum(image * image)), ('freq', 'recv'))  32.6 us
    dot_general x5, matrix products, forward(): jnp.einsum('fbs,frs->fbr', direction[1], imag_operator, preferred_element...  17.2 us
    dot_general x5, matrix products, forward(): jnp.einsum('fbs,frs->fbr', direction[1], real_operator, preferred_element...  17.2 us
    dot_general x5, matrix products, forward(): jnp.einsum('fbs,frs->fbr', direction[0], imag_operator, preferred_element...  17.2 us
  transfers between devices with their start and end apart: 15, of which 15 were waited for; matrix products, arithmetic and copies ran while one was open for 1% of the time, Pallas kernels for 0%

commit v1 on v0

--- a/solution.py
+++ b/solution.py
@@ -7,6 +7,24 @@
 SBLK = 128
 LINK_TYPE = jnp.float32
 ITERS = 5
+
+
+def laid_out(blocks, dim):
+    blocks = jnp.moveaxis(blocks, 0, dim)
+    dims = blocks.shape
+    return blocks.reshape(*dims[:dim], dims[dim] * dims[dim + 1], *dims[dim + 2 :])
+
+
+def doubled_2(value, axis):
+    length = lax.axis_size(axis)
+    parts = value[None]
+    for level in range(length.bit_length() - 1):
+        distance = 1 << level
+        partner_block = lax.ppermute(parts, axis, [(i, i ^ distance) for i in range(length)])
+        both = jnp.stack([parts, partner_block])
+        upper = lax.axis_index(axis) >> level & 1
+        parts = jnp.where(upper == 0, both, both[::-1]).reshape(-1, *value.shape)
+    return parts
 
 
 def high_dot(left, right):
@@ -90,7 +108,7 @@
     pieces = split_parts(values)
     extra = jnp.zeros((16, src_local), jnp.float32).at[0, : pieces.shape[0]].set(pieces)
     payload = jnp.concatenate([rows, extra.astype(jnp.bfloat16)])
-    gathered = lax.all_gather(payload, "recv", axis=1, tiled=True)
+    gathered = laid_out(doubled_2(payload, "recv"), 1)
     count = rows.shape[0]
     half = count // 2
     joined = gathered[:half].astype(jnp.float32) + gathered[half:count].astype(jnp.float32)

time: 644 us -> 701 us (1.089)
  starting transfers between devices: 1.88 us -> 20.5 us
  matrix products: 136 us -> 152 us
  local copies, waits for them, and re-layouts: 21.9 us -> 34.2 us
  waiting for transfers between devices: 353 us -> 365 us
    ppermute x0 -> x10, waiting for transfers between devices: none -> 150 us  [doubled_2(): lax.ppermute(parts, axis, [(i, i ^ distance) for i in range(length)])]
    all_gather x5 -> x0, waiting for transfers between devices: 139 us -> none  [gather_sources(): gathered = lax.all_gather(payload, 'recv', axis=1, tiled=True)]
    ppermute x0 -> x10, starting transfers between devices: none -> 20.1 us  [doubled_2(): lax.ppermute(parts, axis, [(i, i ^ distance) for i in range(length)])]
    dot_general x5, matrix products: 5.64 us -> 14.4 us  [adjoint(): jnp.einsum('fbr,frs->fbs', res[0], imag_operator, preferred_element_type=...]
  transfers between devices with their start and end apart: 15 -> 20, of which waited for: 15 -> 20; matrix products, arithmetic and copies ran while one was open for 1% -> 2% of each run, Pallas kernels for 0% -> 0%
where the time goes in v1:
time: 701 us; the launch traced here: 695 us
  waiting for transfers between devices  365 us (52%)
  matrix products  152 us (22%)
  between operations  62.6 us (9%)
  local copies, waits for them, and re-layouts  34.2 us (5%)
  blocking collectives  33.2 us (5%)
  other arithmetic  28.1 us (4%)
  starting transfers between devices  20.5 us (3%)
    ppermute x10, waiting for transfers between devices, doubled_2(): lax.ppermute(parts, axis, [(i, i ^ distance) for i in range(length)])  150 us
    reduce_scatter x5, waiting for transfers between devices, reduce_gather(): lax.psum_scatter(partial.astype(LINK_TYPE), 'recv', scatter_dimension=3,...  139 us
    all_gather x5, waiting for transfers between devices, reduce_gather(): return lax.all_gather(flat, 'freq', axis=1, tiled=True).astype(jnp.float32)  76.2 us
    dot_general x40, matrix products, high_dot(): return jnp.dot(left, right, precision=lax.Precision.HIGHEST)  54.7 us
    psum x1, blocking collectives, on_device(): lax.psum((own_power, jnp.sum(image * image)), ('freq', 'recv'))  33.2 us
    ppermute x10, starting transfers between devices, doubled_2(): lax.ppermute(parts, axis, [(i, i ^ distance) for i in range(length)])  20.1 us
    dot_general x5, matrix products, forward(): jnp.einsum('fbs,frs->fbr', direction[1], real_operator, preferred_element...  17.6 us
    dot_general x5, matrix products, forward(): jnp.einsum('fbs,frs->fbr', direction[0], imag_operator, preferred_element...  17.4 us
  transfers between devices with their start and end apart: 20, of which 20 were waited for; matrix products, arithmetic and copies ran while one was open for 2% of the time, Pallas kernels for 0%

profile of v1, /device:TPU:0, one launch (start us, length us, event | category | flops | bytes accessed | tf_op | source)
XLA Modules:
  0.0 695.5 jit_solution(3872600486575029293)
XLA Ops:
  8.1 3.0 fusion.38
  11.1 3.4 fusion.40
  17.0 29.9 %reduce-scatter.6.cloned.1.call-done = f32[2,8,8,512]{3,2,1,0:T(8,128)} async-done(((f32[2,8,8,2048]{3,2,1,0:T(8,128)}), f32[2,8,8,512]{3,2,1,0:T(8,128)}) %reduce-scatter.6.cloned.1.call-update) | async-done | bytes 262160 | tf_op jit(solution)/shard_map/reduce_scatter | solution.py:99
  48.9 2.3 select_reduce_fusion.1
  51.2 13.3 %all-gather.6.cloned.1.call-done = f32[2,32,4096]{2,1,0:T(8,128)} async-done(((f32[2,8,4096]{2,1,0:T(8,128)}), f32[2,32,4096]{2,1,0:T(8,128)}) %all-gather.6.cloned.1.call-update) | async-done | bytes 1048592 | tf_op jit(solution)/shard_map/all_gather | solution.py:101
  68.1 1.8 fusion.1
  69.9 2.5 add_reduce_fusion.8
  81.0 7.3 %collective-permute-done = bf16[1,272,512]{2,1,0:T(8,128)(2,1)S(1)} collective-permute-done((bf16[1,272,512]{2,1,0:T(8,128)(2,1)S(1)}, bf16[1,272,512]{2,1,0:T(8,128)(2,1)S(1)}, u32[]{:S(2)}, u32[]{:S(2)}) %collective-permute-start) | collective-permute-done | bytes 278560 | tf_op jit(solution)/shard_map/ppermute | solution.py:23
  88.5 2.5 collective-permute-start.1
  90.9 24.5 %collective-permute-done.1 = bf16[2,272,512]{2,1,0:T(8,128)(2,1)} collective-permute-done((bf16[2,272,512]{2,1,0:T(8,128)(2,1)S(1)}, bf16[2,272,512]{2,1,0:T(8,128)(2,1)}, u32[]{:S(2)}, u32[]{:S(2)}) %collective-permute-start.1) | collective-permute-done | bytes 557088 | tf_op jit(solution)/shard_map/ppermute | solution.py:23
  119.4 3.4 fusion.36
  123.0 3.5 fusion.34
  126.5 3.4 fusion.145
  129.9 3.5 fusion.151
  133.4 2.8 fusion.30
  139.8 27.2 %reduce-scatter.8.cloned.1.call-done = f32[2,8,8,512]{3,2,1,0:T(8,128)} async-done(((f32[2,8,8,2048]{3,2,1,0:T(8,128)}), f32[2,8,8,512]{3,2,1,0:T(8,128)}) %reduce-scatter.8.cloned.1.call-update) | async-done | bytes 262160 | tf_op jit(solution)/shard_map/reduce_scatter | solution.py:99
  168.8 15.6 %all-gather.8.cloned.1.call-done = f32[2,32,4096]{2,1,0:T(8,128)} async-done(((f32[2,8,4096]{2,1,0:T(8,128)}), f32[2,32,4096]{2,1,0:T(8,128)}) %all-gather.8.cloned.1.call-update) | async-done | bytes 1048592 | tf_op jit(solution)/shard_map/all_gather | solution.py:101
  187.9 1.7 convolution_subtract_fusion.3
  189.6 2.4 add_reduce_fusion.7
  201.6 7.3 %collective-permute-done.2 = bf16[1,272,512]{2,1,0:T(8,128)(2,1)S(1)} collective-permute-done((bf16[1,272,512]{2,1,0:T(8,128)(2,1)S(1)}, bf16[1,272,512]{2,1,0:T(8,128)(2,1)S(1)}, u32[]{:S(2)}, u32[]{:S(2)}) %collective-permute-start.2) | collective-permute-done | bytes 278560 | tf_op jit(solution)/shard_map/ppermute | solution.py:23
  209.0 2.5 collective-permute-start.3
  212.8 23.1 %collective-permute-done.3 = bf16[2,272,512]{2,1,0:T(8,128)(2,1)S(1)} collective-permute-done((bf16[2,272,512]{2,1,0:T(8,128)(2,1)S(1)}, bf16[2,272,512]{2,1,0:T(8,128)(2,1)S(1)}, u32[]{:S(2)}, u32[]{:S(2)}) %collective-permute-start.3) | collective-permute-done | bytes 557088 | tf_op jit(solution)/shard_map/ppermute | solution.py:23
  240.0 2.1 fusion.626
  244.3 3.4 fusion.28
  248.8 3.5 fusion.26
  252.4 3.4 fusion.157
  255.7 3.5 fusion.163
  259.3 2.8 fusion.22
  265.9 27.2 %reduce-scatter.10.cloned.1.call-done = f32[2,8,8,512]{3,2,1,0:T(8,128)} async-done(((f32[2,8,8,2048]{3,2,1,0:T(8,128)}), f32[2,8,8,512]{3,2,1,0:T(8,128)}) %reduce-scatter.10.cloned.1.call-update) | async-done | bytes 262160 | tf_op jit(solution)/shard_map/reduce_scatter | solution.py:99
  294.9 15.7 %all-gather.10.cloned.1.call-done = f32[2,32,4096]{2,1,0:T(8,128)} async-done(((f32[2,8,4096]{2,1,0:T(8,128)}), f32[2,32,4096]{2,1,0:T(8,128)}) %all-gather.10.cloned.1.call-update) | async-done | bytes 1048592 | tf_op jit(solution)/shard_map/all_gather | solution.py:101
  314.1 1.8 convolution_subtract_fusion.2
  315.9 3.9 add_reduce_fusion.5
  336.0 7.3 %collective-permute-done.4 = bf16[1,272,512]{2,1,0:T(8,128)(2,1)S(1)} collective-permute-done((bf16[1,272,512]{2,1,0:T(8,128)(2,1)S(1)}, bf16[1,272,512]{2,1,0:T(8,128)(2,1)S(1)}, u32[]{:S(2)}, u32[]{:S(2)}) %collective-permute-start.4) | collective-permute-done | bytes 278560 | tf_op jit(solution)/shard_map/ppermute | solution.py:23
  343.5 2.5 collective-permute-start.5
  345.9 24.4 %collective-permute-done.5 = bf16[2,272,512]{2,1,0:T(8,128)(2,1)S(1)} collective-permute-done((bf16[2,272,512]{2,1,0:T(8,128)(2,1)S(1)}, bf16[2,272,512]{2,1,0:T(8,128)(2,1)S(1)}, u32[]{:S(2)}, u32[]{:S(2)}) %collective-permute-start.5) | collective-permute-done | bytes 557088 | tf_op jit(solution)/shard_map/ppermute | solution.py:23
  376.7 3.4 fusion.20
  380.3 3.5 fusion.18
  383.8 3.4 fusion.169
  387.2 3.5 fusion.175
  390.8 2.8 fusion.14
  397.1 27.2 %reduce-scatter.12.cloned.1.call-done = f32[2,8,8,512]{3,2,1,0:T(8,128)} async-done(((f32[2,8,8,2048]{3,2,1,0:T(8,128)}), f32[2,8,8,512]{3,2,1,0:T(8,128)}) %reduce-scatter.12.cloned.1.call-update) | async-done | bytes 262160 | tf_op jit(solution)/shard_map/reduce_scatter | solution.py:99
  426.1 15.8 %all-gather.12.cloned.1.call-done = f32[2,32,4096]{2,1,0:T(8,128)} async-done(((f32[2,8,4096]{2,1,0:T(8,128)}), f32[2,32,4096]{2,1,0:T(8,128)}) %all-gather.12.cloned.1.call-update) | async-done | bytes 1048592 | tf_op jit(solution)/shard_map/all_gather | solution.py:101
  445.4 1.7 convolution_subtract_fusion.1
  447.2 3.9 add_reduce_fusion.3
  464.8 7.3 %collective-permute-done.6 = bf16[1,272,512]{2,1,0:T(8,128)(2,1)S(1)} collective-permute-done((bf16[1,272,512]{2,1,0:T(8,128)(2,1)S(1)}, bf16[1,272,512]{2,1,0:T(8,128)(2,1)S(1)}, u32[]{:S(2)}, u32[]{:S(2)}) %collective-permute-start.6) | collective-permute-done | bytes 278560 | tf_op jit(solution)/shard_map/ppermute | solution.py:23
  472.3 2.5 collective-permute-start.7
  474.8 24.4 %collective-permute-done.7 = bf16[2,272,512]{2,1,0:T(8,128)(2,1)S(1)} collective-permute-done((bf16[2,272,512]{2,1,0:T(8,128)(2,1)S(1)}, bf16[2,272,512]{2,1,0:T(8,128)(2,1)S(1)}, u32[]{:S(2)}, u32[]{:S(2)}) %collective-permute-start.7) | collective-permute-done | bytes 557088 | tf_op jit(solution)/shard_map/ppermute | solution.py:23
  503.5 3.0 fusion.625
  506.9 3.4 fusion.12
  510.4 3.5 fusion.10
  514.0 3.4 fusion.181
  517.3 3.5 fusion.187
  520.9 2.8 fusion.6
  527.3 27.2 %reduce-scatter.14.cloned.1.call-done = f32[2,8,8,512]{3,2,1,0:T(8,128)} async-done(((f32[2,8,8,2048]{3,2,1,0:T(8,128)}), f32[2,8,8,512]{3,2,1,0:T(8,128)}) %reduce-scatter.14.cloned.1.call-update) | async-done | bytes 262160 | tf_op jit(solution)/shard_map/reduce_scatter | solution.py:99
  556.2 15.7 %all-gather.14.cloned.1.call-done = f32[2,32,4096]{2,1,0:T(8,128)} async-done(((f32[2,8,4096]{2,1,0:T(8,128)}), f32[2,32,4096]{2,1,0:T(8,128)}) %all-gather.14.cloned.1.call-update) | async-done | bytes 1048592 | tf_op jit(solution)/shard_map/all_gather | solution.py:101
  577.2 3.6 add_reduce_fusion.1
  594.5 7.3 %collective-permute-done.8 = bf16[1,272,512]{2,1,0:T(8,128)(2,1)S(1)} collective-permute-done((bf16[1,272,512]{2,1,0:T(8,128)(2,1)S(1)}, bf16[1,272,512]{2,1,0:T(8,128)(2,1)S(1)}, u32[]{:S(2)}, u32[]{:S(2)}) %collective-permute-start.8) | collective-permute-done | bytes 278560 | tf_op jit(solution)/shard_map/ppermute | solution.py:23
  602.8 2.4 collective-permute-start.9
  612.6 17.3 %collective-permute-done.9 = bf16[2,272,512]{2,1,0:T(8,128)(2,1)} collective-permute-done((bf16[2,272,512]{2,1,0:T(8,128)(2,1)}, bf16[2,272,512]{2,1,0:T(8,128)(2,1)}, u32[]{:S(2)}, u32[]{:S(2)}) %collective-permute-start.9) | collective-permute-done | bytes 557088 | tf_op jit(solution)/shard_map/ppermute | solution.py:23
  635.1 3.4 fusion.4
  638.6 3.4 fusion.2
  642.0 3.5 fusion.193
  645.6 3.5 fusion.199
  651.4 33.2 %all-reduce.5 = (f32[]{:T(128)}, f32[]{:T(128)}) all-reduce(f32[]{:T(128)S(6)} %select_n.155, f32[]{:T(128)} %multiply_reduce_fusion), channel_id=1, replica_groups=mesh['groups'=2,'freq'=4,'recv'=4] {'freq','recv'}, use_global_device_ids=true, to_apply=%region_24.25 | all-reduce | flops 2 | bytes 16 | tf_op jit(solution)/shard_map/psum | solution.py:182
  (306 shorter events, 104.7 us)
Async XLA Ops:
  7.2 39.8 %reduce-scatter.6.cloned.1.call-start = ((), (), s32[]{:S(2)}) async-start(), calls=%async_computation.5 | async-start | bytes 1310720 | tf_op jit(solution)/shard_map/reduce_scatter | solution.py:99
  8.1 6.4 copy-start
  15.1 33.6 %copy-start.46 = (s32[8,16]{1,0:T(8,128)S(1)}, s32[8,16]{1,0:T(8,128)}, u32[]{:S(2)}) copy-start(s32[8,16]{1,0:T(8,128)} %param.16) | copy-start | bytes 1540
  15.1 33.7 %copy-start.47 = (s32[8,16]{1,0:T(8,128)S(1)}, s32[8,16]{1,0:T(8,128)}, u32[]{:S(2)}) copy-start(s32[8,16]{1,0:T(8,128)} %param.17) | copy-start | bytes 1540
  17.0 47.6 %all-gather.6.cloned.1.call-start = ((), (), s32[]{:S(2)}) async-start(), calls=%async_computation.6 | async-start | bytes 1310720 | tf_op jit(solution)/shard_map/all_gather | solution.py:101
  48.7 118.3 %reduce-scatter.8.cloned.1.call-start = ((), (), s32[]{:S(2)}) async-start(), calls=%async_computation.7 | async-start | bytes 1310720 | tf_op jit(solution)/shard_map/reduce_scatter | solution.py:99
  79.4 8.9 %collective-permute-start = (bf16[1,272,512]{2,1,0:T(8,128)(2,1)S(1)}, bf16[1,272,512]{2,1,0:T(8,128)(2,1)S(1)}, u32[]{:S(2)}, u32[]{:S(2)}) collective-permute-start(bf16[1,272,512]{2,1,0:T(8,128)(2,1)S(1)} %get-tuple-element.111), channel_id=1, source_target_pairs={{0,1},{1,0},{2,3},{3,2},{4,5},{5,4},{6,7},{7,6},{8,9},{9,8},{10,11... | collective-permute-start | bytes 835592 | tf_op jit(solution)/shard_map/ppermute | solution.py:23
  88.5 27.0 %collective-permute-start.1 = (bf16[2,272,512]{2,1,0:T(8,128)(2,1)S(1)}, bf16[2,272,512]{2,1,0:T(8,128)(2,1)}, u32[]{:S(2)}, u32[]{:S(2)}) collective-permute-start(bf16[2,272,512]{2,1,0:T(8,128)(2,1)S(1)} %get-tuple-element.91), channel_id=1, source_target_pairs={{0,2},{1,3},{2,0},{3,1},{4,6},{5,7},{6,4},{7,5},{8,10},{9,11},{10,... | collective-permute-start | bytes 1671176 | tf_op jit(solution)/shard_map/ppermute | solution.py:23
  123.0 13.3 %slice-start = ((s8[8388608]{0:T(1024)(128)(4,1)}), s8[4194304]{0:T(1024)(128)(4,1)S(1)}, s32[]{:S(2)}) async-start(s8[8388608]{0:T(1024)(128)(4,1)} %bitcast.474), calls=%async_computation.15 | async-start | bytes 8388608
  129.9 6.4 slice-start.1
  139.7 44.7 %all-gather.8.cloned.1.call-start = ((), (), s32[]{:S(2)}) async-start(), calls=%async_computation.8 | async-start | bytes 1310720 | tf_op jit(solution)/shard_map/all_gather | solution.py:101
  168.7 124.4 %reduce-scatter.10.cloned.1.call-start = ((), (), s32[]{:S(2)}) async-start(), calls=%async_computation.9 | async-start | bytes 1310720 | tf_op jit(solution)/shard_map/reduce_scatter | solution.py:99
  192.1 43.9 %copy-start.7 = (f32[32,4096]{1,0:T(8,128)}, f32[32,4096]{1,0:T(8,128)S(1)}, u32[]{:S(2)}) copy-start(f32[32,4096]{1,0:T(8,128)S(1)} %get-tuple-element.141) | copy-start | bytes 1572868
  200.0 8.9 %collective-permute-start.2 = (bf16[1,272,512]{2,1,0:T(8,128)(2,1)S(1)}, bf16[1,272,512]{2,1,0:T(8,128)(2,1)S(1)}, u32[]{:S(2)}, u32[]{:S(2)}) collective-permute-start(bf16[1,272,512]{2,1,0:T(8,128)(2,1)S(1)} %get-tuple-element.109), channel_id=1, source_target_pairs={{0,1},{1,0},{2,3},{3,2},{4,5},{5,4},{6,7},{7,6},{8,9},{9,8},{10,11... | collective-permute-start | bytes 835592 | tf_op jit(solution)/shard_map/ppermute | solution.py:23
  209.0 26.8 %collective-permute-start.3 = (bf16[2,272,512]{2,1,0:T(8,128)(2,1)S(1)}, bf16[2,272,512]{2,1,0:T(8,128)(2,1)S(1)}, u32[]{:S(2)}, u32[]{:S(2)}) collective-permute-start(bf16[2,272,512]{2,1,0:T(8,128)(2,1)S(1)} %get-tuple-element.89), channel_id=1, source_target_pairs={{0,2},{1,3},{2,0},{3,1},{4,6},{5,7},{6,4},{7,5},{8,10},{9,11},{10,... | collective-permute-start | bytes 1671176 | tf_op jit(solution)/shard_map/ppermute | solution.py:23
  248.8 13.3 %slice-start.2 = ((s8[8388608]{0:T(1024)(128)(4,1)}), s8[4194304]{0:T(1024)(128)(4,1)S(1)}, s32[]{:S(2)}) async-start(s8[8388608]{0:T(1024)(128)(4,1)} %bitcast.476), calls=%async_computation.17 | async-start | bytes 8388608
  255.7 6.4 copy-start.37
  255.7 6.4 slice-start.3
  265.8 44.8 %all-gather.10.cloned.1.call-start = ((), (), s32[]{:S(2)}) async-start(), calls=%async_computation.10 | async-start | bytes 1310720 | tf_op jit(solution)/shard_map/all_gather | solution.py:101
  294.8 129.5 %reduce-scatter.12.cloned.1.call-start = ((), (), s32[]{:S(2)}) async-start(), calls=%async_computation.11 | async-start | bytes 1310720 | tf_op jit(solution)/shard_map/reduce_scatter | solution.py:99
  332.5 38.2 %copy-start.19 = (f32[8,4096]{1,0:T(8,128)}, f32[8,4096]{1,0:T(8,128)S(1)}, u32[]{:S(2)}) copy-start(f32[8,4096]{1,0:T(8,128)S(1)} %convolution_subtract_fusion.7) | copy-start | bytes 393220
  334.1 36.5 %copy-start.21 = (f32[8,4096]{1,0:T(8,128)}, f32[8,4096]{1,0:T(8,128)S(1)}, u32[]{:S(2)}) copy-start(f32[8,4096]{1,0:T(8,128)S(1)} %convolution_add_fusion.7) | copy-start | bytes 393220
  334.4 8.9 %collective-permute-start.4 = (bf16[1,272,512]{2,1,0:T(8,128)(2,1)S(1)}, bf16[1,272,512]{2,1,0:T(8,128)(2,1)S(1)}, u32[]{:S(2)}, u32[]{:S(2)}) collective-permute-start(bf16[1,272,512]{2,1,0:T(8,128)(2,1)S(1)} %get-tuple-element.107), channel_id=1, source_target_pairs={{0,1},{1,0},{2,3},{3,2},{4,5},{5,4},{6,7},{7,6},{8,9},{9,8},{10,11... | collective-permute-start | bytes 835592 | tf_op jit(solution)/shard_map/ppermute | solution.py:23
  343.5 26.8 %collective-permute-start.5 = (bf16[2,272,512]{2,1,0:T(8,128)(2,1)S(1)}, bf16[2,272,512]{2,1,0:T(8,128)(2,1)S(1)}, u32[]{:S(2)}, u32[]{:S(2)}) collective-permute-start(bf16[2,272,512]{2,1,0:T(8,128)(2,1)S(1)} %get-tuple-element.87), channel_id=1, source_target_pairs={{0,2},{1,3},{2,0},{3,1},{4,6},{5,7},{6,4},{7,5},{8,10},{9,11},{10,... | collective-permute-start | bytes 1671176 | tf_op jit(solution)/shard_map/ppermute | solution.py:23
  380.3 13.3 %slice-start.4 = ((s8[8388608]{0:T(1024)(128)(4,1)}), s8[4194304]{0:T(1024)(128)(4,1)S(1)}, s32[]{:S(2)}) async-start(s8[8388608]{0:T(1024)(128)(4,1)} %bitcast.478), calls=%async_computation.19 | async-start | bytes 8388608
  387.2 6.4 copy-start.41
  387.2 6.4 slice-start.5
  395.9 51.3 %copy-start.6 = (f32[32,4096]{1,0:T(8,128)S(1)}, f32[32,4096]{1,0:T(8,128)}, u32[]{:S(2)}) copy-start(f32[32,4096]{1,0:T(8,128)} %get-tuple-element.142) | copy-start | bytes 1572868
  397.1 44.8 %all-gather.12.cloned.1.call-start = ((), (), s32[]{:S(2)}) async-start(), calls=%async_computation.12 | async-start | bytes 1310720 | tf_op jit(solution)/shard_map/all_gather | solution.py:101
  426.1 128.4 %reduce-scatter.14.cloned.1.call-start = ((), (), s32[]{:S(2)}) async-start(), calls=%async_computation.13 | async-start | bytes 1310720 | tf_op jit(solution)/shard_map/reduce_scatter | solution.py:99
  451.1 21.1 %copy-start.4 = (f32[32,4096]{1,0:T(8,128)}, f32[32,4096]{1,0:T(8,128)S(1)}, u32[]{:S(2)}) copy-start(f32[32,4096]{1,0:T(8,128)S(1)} %get-tuple-element.143) | copy-start | bytes 1572868
  462.4 9.7 %copy-start.23 = (f32[8,4096]{1,0:T(8,128)}, f32[8,4096]{1,0:T(8,128)S(1)}, u32[]{:S(2)}) copy-start(f32[8,4096]{1,0:T(8,128)S(1)} %convolution_subtract_fusion.6) | copy-start | bytes 393220
  463.0 9.2 %copy-start.24 = (f32[8,4096]{1,0:T(8,128)}, f32[8,4096]{1,0:T(8,128)S(1)}, u32[]{:S(2)}) copy-start(f32[8,4096]{1,0:T(8,128)S(1)} %convolution_add_fusion.6) | copy-start | bytes 393220
  463.2 8.9 %collective-permute-start.6 = (bf16[1,272,512]{2,1,0:T(8,128)(2,1)S(1)}, bf16[1,272,512]{2,1,0:T(8,128)(2,1)S(1)}, u32[]{:S(2)}, u32[]{:S(2)}) collective-permute-start(bf16[1,272,512]{2,1,0:T(8,128)(2,1)S(1)} %get-tuple-element.105), channel_id=1, source_target_pairs={{0,1},{1,0},{2,3},{3,2},{4,5},{5,4},{6,7},{7,6},{8,9},{9,8},{10,11... | collective-permute-start | bytes 835592 | tf_op jit(solution)/shard_map/ppermute | solution.py:23
  472.2 31.3 %copy-start.2 = (bf16[4,272,512]{2,0,1:T(4,128)(2,1)S(1)}, bf16[4,272,512]{2,0,1:T(4,128)(2,1)}, u32[]{:S(2)}) copy-start(bf16[4,272,512]{2,0,1:T(4,128)(2,1)} %copy-done.1) | copy-start | bytes 3342340
  472.3 26.8 %collective-permute-start.7 = (bf16[2,272,512]{2,1,0:T(8,128)(2,1)S(1)}, bf16[2,272,512]{2,1,0:T(8,128)(2,1)S(1)}, u32[]{:S(2)}, u32[]{:S(2)}) collective-permute-start(bf16[2,272,512]{2,1,0:T(8,128)(2,1)S(1)} %get-tuple-element.85), channel_id=1, source_target_pairs={{0,2},{1,3},{2,0},{3,1},{4,6},{5,7},{6,4},{7,5},{8,10},{9,11},{10,... | collective-permute-start | bytes 1671176 | tf_op jit(solution)/shard_map/ppermute | solution.py:23
  510.4 13.3 %slice-start.6 = ((s8[8388608]{0:T(1024)(128)(4,1)}), s8[4194304]{0:T(1024)(128)(4,1)S(1)}, s32[]{:S(2)}) async-start(s8[8388608]{0:T(1024)(128)(4,1)} %bitcast.480), calls=%async_computation.21 | async-start | bytes 8388608
  517.3 6.4 copy-start.44
  517.3 6.4 slice-start.7
  526.1 51.1 %copy-start.5 = (f32[32,4096]{1,0:T(8,128)S(1)}, f32[32,4096]{1,0:T(8,128)}, u32[]{:S(2)}) copy-start(f32[32,4096]{1,0:T(8,128)} %copy-done.4) | copy-start | bytes 1572868
  526.1 51.1 %copy-start.11 = (f32[32,4096]{1,0:T(8,128)S(1)}, f32[32,4096]{1,0:T(8,128)}, u32[]{:S(2)}) copy-start(f32[32,4096]{1,0:T(8,128)} %get-tuple-element.76) | copy-start | bytes 1572868
  526.1 51.2 %copy-start.12 = (f32[32,4096]{1,0:T(8,128)S(1)}, f32[32,4096]{1,0:T(8,128)}, u32[]{:S(2)}) copy-start(f32[32,4096]{1,0:T(8,128)} %get-tuple-element.77) | copy-start | bytes 1572868
  527.2 44.7 %all-gather.14.cloned.1.call-start = ((), (), s32[]{:S(2)}) async-start(), calls=%async_computation.14 | async-start | bytes 1310720 | tf_op jit(solution)/shard_map/all_gather | solution.py:101
  591.0 15.1 %copy-start.16 = (f32[8,4096]{1,0:T(8,128)S(1)}, f32[8,4096]{1,0:T(8,128)}, u32[]{:S(2)}) copy-start(f32[8,4096]{1,0:T(8,128)} %copy-done.15) | copy-start | bytes 393220
  591.0 15.1 %copy-start.18 = (f32[8,4096]{1,0:T(8,128)S(1)}, f32[8,4096]{1,0:T(8,128)}, u32[]{:S(2)}) copy-start(f32[8,4096]{1,0:T(8,128)} %copy-done.17) | copy-start | bytes 393220
  591.0 15.2 %copy-start.20 = (f32[8,4096]{1,0:T(8,128)S(1)}, f32[8,4096]{1,0:T(8,128)}, u32[]{:S(2)}) copy-start(f32[8,4096]{1,0:T(8,128)} %copy-done.19) | copy-start | bytes 393220
  591.5 15.4 %copy-start.22 = (f32[8,4096]{1,0:T(8,128)S(1)}, f32[8,4096]{1,0:T(8,128)}, u32[]{:S(2)}) copy-start(f32[8,4096]{1,0:T(8,128)} %copy-done.21) | copy-start | bytes 393220
  592.1 13.3 %copy-start.27 = (f32[8,4096]{1,0:T(8,128)}, f32[8,4096]{1,0:T(8,128)S(1)}, u32[]{:S(2)}) copy-start(f32[8,4096]{1,0:T(8,128)S(1)} %convolution_subtract_fusion.5) | copy-start | bytes 393220
  592.6 12.8 %copy-start.25 = (f32[8,4096]{1,0:T(8,128)}, f32[8,4096]{1,0:T(8,128)S(1)}, u32[]{:S(2)}) copy-start(f32[8,4096]{1,0:T(8,128)S(1)} %convolution_add_fusion.5) | copy-start | bytes 393220
  592.9 8.9 %collective-permute-start.8 = (bf16[1,272,512]{2,1,0:T(8,128)(2,1)S(1)}, bf16[1,272,512]{2,1,0:T(8,128)(2,1)S(1)}, u32[]{:S(2)}, u32[]{:S(2)}) collective-permute-start(bf16[1,272,512]{2,1,0:T(8,128)(2,1)S(1)} %get-tuple-element.103), channel_id=1, source_target_pairs={{0,1},{1,0},{2,3},{3,2},{4,5},{5,4},{6,7},{7,6},{8,9},{9,8},{10,11... | collective-permute-start | bytes 835592 | tf_op jit(solution)/shard_map/ppermute | solution.py:23
  602.8 27.1 %collective-permute-start.9 = (bf16[2,272,512]{2,1,0:T(8,128)(2,1)}, bf16[2,272,512]{2,1,0:T(8,128)(2,1)}, u32[]{:S(2)}, u32[]{:S(2)}) collective-permute-start(bf16[2,272,512]{2,1,0:T(8,128)(2,1)} %get-tuple-element.83), channel_id=1, source_target_pairs={{0,2},{1,3},{2,0},{3,1},{4,6},{5,7},{6,4},{7,5},{8,10},{9,11},{10,... | collective-permute-start | bytes 1671176 | tf_op jit(solution)/shard_map/ppermute | solution.py:23
  606.1 28.1 %copy-start.10 = (f32[128,4,512]{2,1,0:T(4,128)S(1)}, f32[128,4,512]{2,1,0:T(4,128)}, u32[]{:S(2)}) copy-start(f32[128,4,512]{2,1,0:T(4,128)} %get-tuple-element.75) | copy-start | bytes 3145732
  642.0 7.0 %copy-start.13 = (f32[32,4096]{1,0:T(8,128)S(1)}, f32[32,4096]{1,0:T(8,128)}, u32[]{:S(2)}) copy-start(f32[32,4096]{1,0:T(8,128)} %get-tuple-element.72) | copy-start | bytes 1572868
  642.0 7.0 %copy-start.14 = (f32[32,4096]{1,0:T(8,128)S(1)}, f32[32,4096]{1,0:T(8,128)}, u32[]{:S(2)}) copy-start(f32[32,4096]{1,0:T(8,128)} %get-tuple-element.73) | copy-start | bytes 1572868
  645.5 40.4 %copy-start.36 = (f32[1,8,8,128]{3,2,1,0:T(8,128)S(1)}, f32[1,8,8,128]{3,2,1,0:T(8,128)}, u32[]{:S(2)}) copy-start(f32[1,8,8,128]{3,2,1,0:T(8,128)} %copy-done.35) | copy-start | bytes 98308
  645.5 40.5 %copy-start.38 = (f32[1,8,8,128]{3,2,1,0:T(8,128)S(1)}, f32[1,8,8,128]{3,2,1,0:T(8,128)}, u32[]{:S(2)}) copy-start(f32[1,8,8,128]{3,2,1,0:T(8,128)} %copy-done.37) | copy-start | bytes 98308
  645.5 40.5 %copy-start.40 = (f32[1,8,8,128]{3,2,1,0:T(8,128)S(1)}, f32[1,8,8,128]{3,2,1,0:T(8,128)}, u32[]{:S(2)}) copy-start(f32[1,8,8,128]{3,2,1,0:T(8,128)} %copy-done.39) | copy-start | bytes 98308
  645.5 40.4 %copy-start.42 = (f32[1,8,8,128]{3,2,1,0:T(8,128)S(1)}, f32[1,8,8,128]{3,2,1,0:T(8,128)}, u32[]{:S(2)}) copy-start(f32[1,8,8,128]{3,2,1,0:T(8,128)} %copy-done.41) | copy-start | bytes 98308
  645.5 42.0 %copy-start.29 = (f32[2,8,8,512]{3,2,1,0:T(8,128)S(1)}, f32[2,8,8,512]{3,2,1,0:T(8,128)}, u32[]{:S(2)}) copy-start(f32[2,8,8,512]{3,2,1,0:T(8,128)} %copy-done.28) | copy-start | bytes 786436
  645.5 42.0 %copy-start.30 = (f32[1,8,8,512]{3,2,1,0:T(8,128)S(1)}, f32[1,8,8,512]{3,2,1,0:T(8,128)}, u32[]{:S(2)}) copy-start(f32[1,8,8,512]{3,2,1,0:T(8,128)} %copy.39) | copy-start | bytes 393220
  645.5 42.0 %copy-start.31 = (f32[1,8,8,512]{3,2,1,0:T(8,128)S(1)}, f32[1,8,8,512]{3,2,1,0:T(8,128)}, u32[]{:S(2)}) copy-start(f32[1,8,8,512]{3,2,1,0:T(8,128)} %copy.38) | copy-start | bytes 393220
  645.6 42.0 %copy-start.32 = (f32[1,8,8,512]{3,2,1,0:T(8,128)S(1)}, f32[1,8,8,512]{3,2,1,0:T(8,128)}, u32[]{:S(2)}) copy-start(f32[1,8,8,512]{3,2,1,0:T(8,128)} %copy.43) | copy-start | bytes 393220
  645.6 42.0 %copy-start.33 = (f32[1,8,8,512]{3,2,1,0:T(8,128)S(1)}, f32[1,8,8,512]{3,2,1,0:T(8,128)}, u32[]{:S(2)}) copy-start(f32[1,8,8,512]{3,2,1,0:T(8,128)} %copy.42) | copy-start | bytes 393220
  645.6 42.0 %copy-start.34 = (f32[1,8,8,512]{3,2,1,0:T(8,128)S(1)}, f32[1,8,8,512]{3,2,1,0:T(8,128)}, u32[]{:S(2)}) copy-start(f32[1,8,8,512]{3,2,1,0:T(8,128)} %copy.45) | copy-start | bytes 393220
  (12 other events, 26.6 us)
Sparse Core Ops, SparseCore 0:
  17.1 29.8 reduce-scatter.5
  49.2 15.3 all-gather.5
  139.8 27.1 reduce-scatter.7
  169.0 15.3 all-gather.7
  266.0 27.1 reduce-scatter.9
  295.2 15.3 all-gather.9
  397.2 27.1 reduce-scatter.11
  426.5 15.3 all-gather.11
  527.3 27.1 reduce-scatter.13
  556.6 15.3 all-gather.13
